TPU v7x, 128 devices: a whole 4x4x4 slice. The times are simulated.
128 devices in a mesh: grp: 8 (over x, core), blk: 16 (over y, z).
Axes of the slice: x: 4, y: 4, z: 4, core: 2. Of those that a mesh axis runs over, the one named last changes fastest.
Arguments:
- features: bfloat16 [8, 16, 4096, 256], P('grp', 'blk'), may hold values from -6 to 6
- hub_rows: int32 [8, 16, 32], P('grp', 'blk'), may hold values from 0 to 4095
- hub_adjacency: bfloat16 [8, 16, 4096, 512], P('grp', 'blk'), as said below
- tile_row: int32 [8, 16, 160], P('grp', 'blk'), may hold values from 0 to 31
- tile_col: int32 [8, 16, 160], P('grp', 'blk'), may hold values from 0 to 63
- tile_count: int32 [8, 16], P('grp', 'blk'), may hold values from 26 to 160, as said below
- tile_values: bfloat16 [8, 16, 160, 128, 128], P('grp', 'blk'), may hold values from 0 to 0.049804688
- send_rows: int32 [8, 16, 8, 16, 32], P('grp', 'blk'), may hold values from 0 to 4095
- weight: bfloat16 [256, 256], replicated, may hold values from -0.375 to 0.375
Outputs:
- activations: bfloat16 [8, 16, 4096, 256], P('grp', 'blk')
Inputs may be any that keep to these rules, and one draw needn't show every extreme that they name: `tile_count`: some device has exactly 160 live tile slots in every draw. `hub_adjacency`: Non-negative edge weights.
All inputs are finite; a program needn't handle non-finite values.
Results may differ from a plain program's by a relative error of at most 0.0014.
The roundings to bfloat16 on the way count: a program that leaves them out, or rounds other values in their place, can miss the bound.
Values may be sent and summed in bfloat16 or wider, within the bound.
No kernel may reach another device: no remote copies, remote signals or barrier semaphores. Data moves between devices by JAX's collectives and lax.ppermute only.
A program may use at most 128 MiB of HBM per device.

v0:
```python
import jax
import jax.numpy as jnp
from jax import lax
from jax.sharding import PartitionSpec as P

TB = 128


def per_device(
    features,
    hub_rows,
    hub_adjacency,
    tile_row,
    tile_col,
    tile_count,
    tile_values,
    send_rows,
    weight,
):
    local = features[0, 0]
    rows = local.shape[0]
    width = local.shape[1]
    adjacency = hub_adjacency[0, 0]
    hub_block = local[hub_rows[0, 0]]
    hub_part = jnp.dot(
        adjacency,
        lax.all_gather(hub_block, "blk", axis=0, tiled=True),
        preferred_element_type=jnp.float32,
    )
    listing = send_rows[0, 0]
    outgoing = local[listing.reshape(-1)]
    incoming = lax.all_to_all(outgoing, ("grp", "blk"), split_axis=0, concat_axis=0, tiled=True)
    table = jnp.concatenate([local, incoming], 0)
    table_blocks = table.shape[0] // TB
    flat_table = table.reshape(table_blocks, TB * width)
    slots = tile_col.shape[-1]
    selector = (
        tile_col[0, 0][:, None] == jnp.arange(table_blocks, dtype=jnp.int32)[None, :]
    ).astype(jnp.bfloat16)
    picked = jnp.dot(selector, flat_table, preferred_element_type=jnp.float32).astype(jnp.bfloat16)
    picked = picked.reshape(slots, TB, width)
    products = jnp.einsum(
        "tij,tjf->tif", tile_values[0, 0], picked, preferred_element_type=jnp.float32
    )
    row_blocks = rows // TB
    valid = jnp.arange(slots, dtype=jnp.int32) < tile_count[0, 0]
    placing = (
        (jnp.arange(row_blocks, dtype=jnp.int32)[:, None] == tile_row[0, 0][None, :])
        & valid[None, :]
    ).astype(jnp.float32)
    tile_part = jnp.dot(
        placing,
        products.reshape(slots, TB * width),
        precision=lax.Precision.HIGHEST,
        preferred_element_type=jnp.float32,
    )
    aggregated = (hub_part + tile_part.reshape(rows, width)).astype(jnp.bfloat16)
    mixed = jnp.dot(aggregated, weight, preferred_element_type=jnp.float32)
    return jnp.maximum(mixed, 0.0).astype(jnp.bfloat16)[None, None]


def solution(mesh):
    return jax.shard_map(
        per_device,
        mesh=mesh,
        in_specs=(
            P("grp", "blk", None, None),
            P("grp", "blk", None),
            P("grp", "blk", None, None),
            P("grp", "blk", None),
            P("grp", "blk", None),
            P("grp", "blk"),
            P("grp", "blk", None, None, None),
            P("grp", "blk", None, None, None),
            P(),
        ),
        out_specs=P("grp", "blk", None, None),
        check_vma=False,
    )
```

profile of v0, /device:TPU:4, one launch (start us, length us, event | category | flops | bytes accessed | tf_op | source)
XLA Modules:
  0.0 164.9 jit_solution(14965506577353493030)
XLA Ops:
  0.0 0.0 copy-start
  0.0 1.0 reshape_squeeze.3
  1.0 17.8 %gather_fusion.1 = bf16[4096,256]{1,0:T(8,128)(2,1)} fusion(bf16[4096,256]{1,0:T(8,128)(2,1)} %bitcast.45, s32[4096]{0:T(1024)S(1)} %broadcast_clamp_fusion), kind=kCustom, calls=%fused_computation.1 | custom fusion | bytes 4210688 | tf_op jit(solution)/shard_map/gather | solution.py:31
  18.8 0.0 copy-start.4
  18.8 0.0 copy-start.1
  18.8 11.0 %all-to-all-start = ((bf16[128,32,256]{2,1,0:T(8,128)(2,1)}), bf16[128,32,256]{2,1,0:T(8,128)(2,1)}, u32[]{:S(2)}, u32[]{:S(2)}) async-start(bf16[128,32,256]{2,1,0:T(8,128)(2,1)} %bitcast.51), calls=%async_computation | async-start | bytes 4194304 | tf_op jit(solution)/shard_map/all_to_all | solution.py:32
  30.4 0.0 copy-done.4
  30.5 0.0 copy-done.1
  30.5 0.6 gather_fusion
  31.1 42.1 %all-gather = bf16[512,256]{1,0:T(8,128)(2,1)S(1)} all-gather(bf16[32,256]{1,0:T(8,128)(2,1)S(1)} %gather_fusion), channel_id=2, replica_groups=mesh['grp'=8,'blk'=16] {'blk'}, dimensions={0}, use_global_device_ids=true | all-gather | bytes 278528 | tf_op jit(solution)/shard_map/all_gather | solution.py:27
  73.2 0.0 all-to-all-done
  73.2 3.8 %pad_maximum_fusion = bf16[8192,256]{1,0:T(8,128)(2,1)} fusion(bf16[4096,256]{1,0:T(8,128)(2,1)} %bitcast.10, bf16[4096,256]{1,0:T(8,128)(2,1)S(1)} %bitcast.47), kind=kLoop, calls=%fused_computation.11 | loop fusion | flops 8388608 | bytes 8388608 | tf_op jit(solution)/shard_map/concatenate | solution.py:33
  77.0 0.0 copy-start.2
  77.0 7.4 %reshape.76 = bf16[64,32768]{1,0:T(8,128)(2,1)} reshape(bf16[8192,256]{1,0:T(8,128)(2,1)} %pad_maximum_fusion) | data formatting | bytes 8388608 | tf_op jit(solution)/shard_map/reshape | solution.py:35
  84.4 0.0 copy-done.2
  84.4 7.7 %convolution_convert_fusion = bf16[160,32768]{1,0:T(8,128)(2,1)} fusion(bf16[64,32768]{1,0:T(8,128)(2,1)} %reshape.76, s32[160]{0:T(256)S(1)} %bitcast.53), kind=kOutput, calls=%fused_computation.2 | convolution fusion | flops 676341760 | bytes 14680704 | tf_op jit(solution)/shard_map/dot_general | solution.py:40
  92.1 11.2 %copy.14 = bf16[20,8,128,256]{3,2,1,0:T(8,128)(2,1)} copy(bf16[20,8,128,256]{3,1,2,0:T(8,128)(2,1)} %bitcast.50) | data formatting | bytes 20971520
  103.4 15.6 %convolution_bitcast_fusion = f32[160,128,256]{1,2,0:T(8,128)} fusion(bf16[160,128,256]{2,1,0:T(8,128)(2,1)} %bitcast.48, bf16[1,1,160,128,128]{4,3,2,1,0:T(8,128)(2,1)} %param.15), kind=kOutput, calls=%fused_computation.3 | convolution fusion | flops 1342177280 | bytes 36700160 | tf_op jit(solution)/shard_map/tij,tjf->tif/dot_general | solution.py:42
  119.0 21.3 %copy.15 = f32[20,8,128,256]{3,1,2,0:T(8,128)} copy(f32[20,8,128,256]{2,3,1,0:T(8,128)} %bitcast.44) | data formatting | bytes 41943040
  140.3 0.0 copy-done.3
  140.3 13.0 %fusion.10 = f32[32,32768]{1,0:T(8,128)} fusion(f32[160,32768]{1,0:T(8,128)} %bitcast.49, s32[160]{0:T(256)S(1)} %bitcast.54, pred[160]{0:T(512)(128)(4,1)S(1)} %iota_compare_fusion.3), kind=kOutput, calls=%fused_computation.18 | convolution fusion | flops 2013276160 | bytes 25166624 | tf_op jit(solution)/shard_map/dot_general | solution.py:51
  153.2 4.9 %reshape.79 = f32[4096,256]{1,0:T(8,128)} reshape(f32[32,32768]{1,0:T(8,128)} %fusion.10) | data formatting | bytes 8388608 | tf_op jit(solution)/shard_map/reshape | solution.py:57
  158.1 0.0 copy-done
  158.1 6.7 %fusion.4 = bf16[1,1,4096,256]{3,2,1,0:T(8,128)(2,1)} fusion(bf16[256,256]{1,0:T(8,128)(2,1)S(1)} %copy-done, f32[4096,256]{1,0:T(8,128)} %reshape.79, bf16[512,256]{1,0:T(8,128)(2,1)S(1)} %all-gather, bf16[1,1,4096,512]{3,2,1,0:T(8,128)(2,1)} %param.11), kind=kOutput, calls=%fused_computation.10 | convolution fusion | flops 1614807040 | bytes 10878976 | tf_op jit(solution)/shard_map/dot_general | solution.py:58
  (6 shorter events, 0.0 us)
Async XLA Ops:
  0.0 158.1 %copy-start = (bf16[256,256]{1,0:T(8,128)(2,1)S(1)}, bf16[256,256]{1,0:T(8,128)(2,1)}, u32[]{:S(2)}) copy-start(bf16[256,256]{1,0:T(8,128)(2,1)} %param.17) | copy-start | bytes 393220
  18.8 11.6 %copy-start.4 = (s32[1,1,32]{2,1,0:T(1,128)S(1)}, s32[1,1,32]{2,1,0:T(1,128)}, u32[]{:S(2)}) copy-start(s32[1,1,32]{2,1,0:T(1,128)} %param.10) | copy-start | bytes 388
  18.8 11.7 %copy-start.1 = (bf16[1,1,4096,256]{3,2,1,0:T(8,128)(2,1)S(1)}, bf16[1,1,4096,256]{3,2,1,0:T(8,128)(2,1)}, u32[]{:S(2)}) copy-start(bf16[1,1,4096,256]{3,2,1,0:T(8,128)(2,1)} %param.9) | copy-start | bytes 6291460
  18.8 54.4 %all-to-all-start = ((bf16[128,32,256]{2,1,0:T(8,128)(2,1)}), bf16[128,32,256]{2,1,0:T(8,128)(2,1)}, u32[]{:S(2)}, u32[]{:S(2)}) async-start(bf16[128,32,256]{2,1,0:T(8,128)(2,1)} %bitcast.51), calls=%async_computation | async-start | bytes 4194304 | tf_op jit(solution)/shard_map/all_to_all | solution.py:32
  77.0 7.4 %copy-start.2 = (s32[1,1,160]{2,1,0:T(1,128)S(1)}, s32[1,1,160]{2,1,0:T(1,128)}, u32[]{:S(2)}) copy-start(s32[1,1,160]{2,1,0:T(1,128)} %param.13) | copy-start | bytes 1924
  119.0 21.3 %copy-start.3 = (s32[1,1,160]{2,1,0:T(1,128)S(1)}, s32[1,1,160]{2,1,0:T(1,128)}, u32[]{:S(2)}) copy-start(s32[1,1,160]{2,1,0:T(1,128)} %param.12) | copy-start | bytes 1924
where the time goes:
time: 166 us; the launch traced here: 165 us
  local copies, waits for them, and re-layouts  64.3 us (39%)
  matrix products  43 us (26%)
  blocking collectives  42.1 us (25%)
  starting transfers between devices  11 us (7%)
  other arithmetic  3.85 us (2%)
    all_gather x1, blocking collectives, per_device(): lax.all_gather(hub_block, 'blk', axis=0, tiled=True)  42.1 us
    unnamed x12, local copies, waits for them, and re-layouts  32.6 us
    gather x1, local copies, waits for them, and re-layouts, per_device(): outgoing = local[listing.reshape(-1)]  17.8 us
    dot_general x1, matrix products, per_device(): jnp.einsum('tij,tjf->tif', tile_values[0, 0], picked, preferred_element_t...  15.6 us
    dot_general x1, matrix products, per_device(): jnp.dot(placing, products.reshape(slots, TB * width), precision=lax.Preci...  13 us
    all_to_all x1, starting transfers between devices, per_device(): lax.all_to_all(outgoing, ('grp', 'blk'), split_axis=0, concat_axis=0, til...  11 us
    dot_general x1, matrix products, per_device(): jnp.dot(selector, flat_table, preferred_element_type=jnp.float32)  7.73 us
    reshape x1, local copies, waits for them, and re-layouts, per_device(): flat_table = table.reshape(table_blocks, TB * width)  7.38 us
  transfers between devices with their start and end apart: 1, of which 0 were waited for; matrix products, arithmetic and copies ran while one was open for 0% of the time, Pallas kernels for 0%

commit v1 on v0

--- a/solution.py
+++ b/solution.py
@@ -24,7 +24,12 @@
     hub_block = local[hub_rows[0, 0]]
     hub_part = jnp.dot(
         adjacency,
-        lax.all_gather(hub_block, "blk", axis=0, tiled=True),
+        jnp.concatenate(
+            jax.lax.all_to_all(
+                jnp.stack([hub_block for _ in range(jax.lax.axis_size("blk"))]), "blk", 0, 0
+            ),
+            axis=0,
+        ),
         preferred_element_type=jnp.float32,
     )
     listing = send_rows[0, 0]

time: 166 us -> 157 us (0.946)
  the two profiles are of different devices: /device:TPU:4 before, /device:TPU:1 now
where the time goes in v1:
time: 157 us; the launch traced here: 156 us
  local copies, waits for them, and re-layouts  65 us (41%)
  matrix products  42.9 us (27%)
  waiting for transfers between devices  27.8 us (18%)
  starting transfers between devices  15.6 us (10%)
  other arithmetic  3.84 us (2%)
    unnamed x12, local copies, waits for them, and re-layouts  32.6 us
    all_to_all x1, waiting for transfers between devices, per_device(): lax.all_to_all(outgoing, ('grp', 'blk'), split_axis=0, concat_axis=0, til...  27.8 us
    gather x1, local copies, waits for them, and re-layouts, per_device(): outgoing = local[listing.reshape(-1)]  17.8 us
    dot_general x1, matrix products, per_device(): jnp.einsum('tij,tjf->tif', tile_values[0, 0], picked, preferred_element_t...  15.6 us
    dot_general x1, matrix products, per_device(): jnp.dot(placing, products.reshape(slots, TB * width), precision=lax.Preci...  12.9 us
    all_to_all x1, starting transfers between devices, per_device(): lax.all_to_all(outgoing, ('grp', 'blk'), split_axis=0, concat_axis=0, til...  12 us
    dot_general x1, matrix products, per_device(): jnp.dot(selector, flat_table, preferred_element_type=jnp.float32)  7.74 us
    reshape x1, local copies, waits for them, and re-layouts, per_device(): flat_table = table.reshape(table_blocks, TB * width)  7.38 us
  transfers between devices with their start and end apart: 2, of which 1 were waited for; matrix products, arithmetic and copies ran while one was open for 55% of the time, Pallas kernels for 0%

profile of v1, /device:TPU:1, one launch (start us, length us, event | category | flops | bytes accessed | tf_op | source)
XLA Modules:
  0.0 155.9 jit_solution(17634149074771361423)
XLA Ops:
  0.0 0.0 copy-start
  0.0 1.0 reshape_squeeze.3
  1.0 17.8 %gather_fusion.1 = bf16[4096,256]{1,0:T(8,128)(2,1)} fusion(bf16[4096,256]{1,0:T(8,128)(2,1)} %bitcast.46, s32[4096]{0:T(1024)S(1)} %broadcast_clamp_fusion), kind=kCustom, calls=%fused_computation.1 | custom fusion | bytes 4210688 | tf_op jit(solution)/shard_map/gather | solution.py:36
  18.8 0.0 copy-start.4
  18.8 12.0 %all-to-all-start.1 = ((bf16[128,32,256]{2,1,0:T(8,128)(2,1)}), bf16[128,32,256]{2,1,0:T(8,128)(2,1)}, u32[]{:S(2)}, u32[]{:S(2)}) async-start(bf16[128,32,256]{2,1,0:T(8,128)(2,1)} %bitcast.52), calls=%async_computation.1 | async-start | bytes 4194304 | tf_op jit(solution)/shard_map/all_to_all | solution.py:37
  31.4 0.0 copy-done.4
  31.5 0.0 copy-done.1
  31.5 0.6 gather_fusion
  32.1 27.8 %all-to-all-done.1 = bf16[128,32,256]{2,1,0:T(8,128)(2,1)} async-done(((bf16[128,32,256]{2,1,0:T(8,128)(2,1)}), bf16[128,32,256]{2,1,0:T(8,128)(2,1)}, u32[]{:S(2)}, u32[]{:S(2)}) %all-to-all-start.1) | async-done | bytes 2097184 | tf_op jit(solution)/shard_map/all_to_all | solution.py:37
  59.9 0.7 stack.2
  60.7 3.7 %all-to-all-start = ((bf16[16,32,256]{2,1,0:T(8,128)(2,1)}), bf16[16,32,256]{2,1,0:T(8,128)(2,1)S(1)}, u32[]{:S(2)}, u32[]{:S(2)}) async-start(bf16[16,32,256]{2,1,0:T(8,128)(2,1)} %stack.2), calls=%async_computation | async-start | bytes 524288 | tf_op jit(solution)/shard_map/all_to_all | solution.py:28
  64.3 3.8 %pad_maximum_fusion = bf16[8192,256]{1,0:T(8,128)(2,1)} fusion(bf16[4096,256]{1,0:T(8,128)(2,1)} %bitcast.11, bf16[4096,256]{1,0:T(8,128)(2,1)S(1)} %bitcast.48), kind=kLoop, calls=%fused_computation.11 | loop fusion | flops 8388608 | bytes 8388608 | tf_op jit(solution)/shard_map/concatenate | solution.py:38
  68.1 7.4 %reshape.82 = bf16[64,32768]{1,0:T(8,128)(2,1)} reshape(bf16[8192,256]{1,0:T(8,128)(2,1)} %pad_maximum_fusion) | data formatting | bytes 8388608 | tf_op jit(solution)/shard_map/reshape | solution.py:40
  75.5 0.0 copy-done.2
  75.5 7.7 %convolution_convert_fusion = bf16[160,32768]{1,0:T(8,128)(2,1)} fusion(bf16[64,32768]{1,0:T(8,128)(2,1)} %reshape.82, s32[160]{0:T(256)S(1)} %bitcast.55), kind=kOutput, calls=%fused_computation.2 | convolution fusion | flops 676341760 | bytes 14680704 | tf_op jit(solution)/shard_map/dot_general | solution.py:45
  83.3 11.2 %copy.14 = bf16[20,8,128,256]{3,2,1,0:T(8,128)(2,1)} copy(bf16[20,8,128,256]{3,1,2,0:T(8,128)(2,1)} %bitcast.51) | data formatting | bytes 20971520
  94.5 15.6 %convolution_bitcast_fusion = f32[160,128,256]{1,2,0:T(8,128)} fusion(bf16[160,128,256]{2,1,0:T(8,128)(2,1)} %bitcast.49, bf16[1,1,160,128,128]{4,3,2,1,0:T(8,128)(2,1)} %param.15), kind=kOutput, calls=%fused_computation.3 | convolution fusion | flops 1342177280 | bytes 36700160 | tf_op jit(solution)/shard_map/tij,tjf->tif/dot_general | solution.py:47
  110.1 21.3 %copy.15 = f32[20,8,128,256]{3,1,2,0:T(8,128)} copy(f32[20,8,128,256]{2,3,1,0:T(8,128)} %bitcast.45) | data formatting | bytes 41943040
  131.4 0.0 copy-done.3
  131.4 12.9 %fusion.10 = f32[32,32768]{1,0:T(8,128)} fusion(f32[160,32768]{1,0:T(8,128)} %bitcast.50, s32[160]{0:T(256)S(1)} %bitcast.56, pred[160]{0:T(512)(128)(4,1)S(1)} %iota_compare_fusion.3), kind=kOutput, calls=%fused_computation.18 | convolution fusion | flops 2013276160 | bytes 25166624 | tf_op jit(solution)/shard_map/dot_general | solution.py:56
  144.3 4.9 %reshape.85 = f32[4096,256]{1,0:T(8,128)} reshape(f32[32,32768]{1,0:T(8,128)} %fusion.10) | data formatting | bytes 8388608 | tf_op jit(solution)/shard_map/reshape | solution.py:62
  149.2 0.0 all-to-all-done
  149.2 0.0 copy-done
  149.2 6.7 %fusion.4 = bf16[1,1,4096,256]{3,2,1,0:T(8,128)(2,1)} fusion(bf16[256,256]{1,0:T(8,128)(2,1)S(1)} %copy-done, f32[4096,256]{1,0:T(8,128)} %reshape.85, bf16[512,256]{1,0:T(8,128)(2,1)S(1)} %bitcast.53, bf16[1,1,4096,512]{3,2,1,0:T(8,128)(2,1)} %param.11), kind=kOutput, calls=%fused_computation.10 | convolution fusion | flops 1614807040 | bytes 10878976 | tf_op jit(solution)/shard_map/dot_general | solution.py:63
  (8 shorter events, 0.0 us)
Async XLA Ops:
  0.0 149.2 %copy-start = (bf16[256,256]{1,0:T(8,128)(2,1)S(1)}, bf16[256,256]{1,0:T(8,128)(2,1)}, u32[]{:S(2)}) copy-start(bf16[256,256]{1,0:T(8,128)(2,1)} %param.17) | copy-start | bytes 393220
  18.8 12.6 %copy-start.4 = (s32[1,1,32]{2,1,0:T(1,128)S(1)}, s32[1,1,32]{2,1,0:T(1,128)}, u32[]{:S(2)}) copy-start(s32[1,1,32]{2,1,0:T(1,128)} %param.10) | copy-start | bytes 388
  18.8 12.7 %copy-start.1 = (bf16[1,1,4096,256]{3,2,1,0:T(8,128)(2,1)S(1)}, bf16[1,1,4096,256]{3,2,1,0:T(8,128)(2,1)}, u32[]{:S(2)}) copy-start(bf16[1,1,4096,256]{3,2,1,0:T(8,128)(2,1)} %param.9) | copy-start | bytes 6291460
  18.8 41.1 %all-to-all-start.1 = ((bf16[128,32,256]{2,1,0:T(8,128)(2,1)}), bf16[128,32,256]{2,1,0:T(8,128)(2,1)}, u32[]{:S(2)}, u32[]{:S(2)}) async-start(bf16[128,32,256]{2,1,0:T(8,128)(2,1)} %bitcast.52), calls=%async_computation.1 | async-start | bytes 4194304 | tf_op jit(solution)/shard_map/all_to_all | solution.py:37
  60.7 88.6 %all-to-all-start = ((bf16[16,32,256]{2,1,0:T(8,128)(2,1)}), bf16[16,32,256]{2,1,0:T(8,128)(2,1)S(1)}, u32[]{:S(2)}, u32[]{:S(2)}) async-start(bf16[16,32,256]{2,1,0:T(8,128)(2,1)} %stack.2), calls=%async_computation | async-start | bytes 524288 | tf_op jit(solution)/shard_map/all_to_all | solution.py:28
  68.1 7.4 %copy-start.2 = (s32[1,1,160]{2,1,0:T(1,128)S(1)}, s32[1,1,160]{2,1,0:T(1,128)}, u32[]{:S(2)}) copy-start(s32[1,1,160]{2,1,0:T(1,128)} %param.13) | copy-start | bytes 1924
  110.1 21.3 %copy-start.3 = (s32[1,1,160]{2,1,0:T(1,128)S(1)}, s32[1,1,160]{2,1,0:T(1,128)}, u32[]{:S(2)}) copy-start(s32[1,1,160]{2,1,0:T(1,128)} %param.12) | copy-start | bytes 1924
